TPU v7x, 256 devices: a whole 4x4x8 slice. The times are simulated.
256 devices in a mesh: seq: 32 (over x_hi, z, core), tp: 8 (over y, x_lo).
Axes of the slice: x: 4 (x_hi: 2, x_lo: 2; x = x_hi * 2 + x_lo), y: 4, z: 8, core: 2. Of those that a mesh axis runs over, the one named last changes fastest.
Arguments:
- proj: bfloat16 [4096, 3, 8192], P('seq', None, 'tp'), may hold values from -6 to 6
- cotangent: bfloat16 [4096, 8192], P('seq', 'tp'), may hold values from -6 to 6
- out_weight: bfloat16 [8192, 8192], P('seq', 'tp'), may hold values from -0.125 to 0.125
- short_weight: float32 [7, 3, 8192], P(None, None, 'tp'), may hold values from -2 to 2
- long_filter: float32 [4096, 8192], P('seq', 'tp')
Outputs:
- grad_proj: bfloat16 [4096, 3, 8192], P('seq', None, 'tp')
- grad_short: float32 [7, 3, 8192], P(None, None, 'tp')
- grad_filter: float32 [4096, 8192], P('seq', 'tp')
All inputs are finite; a program needn't handle non-finite values.
Results may differ from a plain program's by a relative error of at most 0.025.
Values may be sent and summed in bfloat16 or wider, within the bound.
No kernel may reach another device: no remote copies, remote signals or barrier semaphores. Data moves between devices by JAX's collectives and lax.ppermute only.
A program may use at most 128 MiB of HBM per device.

v0:
```python
import math
import jax
import jax.numpy as jnp
from jax import lax
from jax.sharding import PartitionSpec as P

highest = lax.Precision.HIGHEST


def shifted(value, axis, by):
    devices = lax.axis_size(axis)
    pairs = [(i, i + by) for i in range(devices) if 0 <= i + by < devices]
    return lax.ppermute(value, axis, pairs)


def angle_tables(row_count, col_count, modulus):
    row_index = jnp.arange(row_count, dtype=jnp.int32)[:, None]
    col_index = jnp.arange(col_count, dtype=jnp.int32)[None, :]
    phase = (row_index * col_index % modulus).astype(jnp.float32) * (2.0 * math.pi / modulus)
    return (jnp.cos(phase), jnp.sin(phase))


def split_length(length):
    whole_len = 2 * length
    ceiling = 1 << whole_len.bit_length() // 2 - 1
    first_len = 2 * math.gcd(length, ceiling)
    return (first_len, whole_len // first_len)


def spectrum(columns):
    length, channels = columns.shape
    first_len, second_len = split_length(length)
    lower_half = first_len // 2
    whole_len = first_len * second_len
    values = columns.astype(jnp.float32).reshape(lower_half, second_len * channels)
    cos_first, sin_first = angle_tables(first_len, lower_half, first_len)
    real_one = jnp.dot(cos_first, values, precision=highest).reshape(
        first_len, second_len, channels
    )
    imag_one = -jnp.dot(sin_first, values, precision=highest).reshape(
        first_len, second_len, channels
    )
    twist_cos, twist_sin = angle_tables(first_len, second_len, whole_len)
    twist_cos = twist_cos[:, :, None]
    twist_sin = twist_sin[:, :, None]
    real_two = real_one * twist_cos + imag_one * twist_sin
    imag_two = imag_one * twist_cos - real_one * twist_sin
    cos_second, sin_second = angle_tables(second_len, second_len, second_len)
    real_out = jnp.einsum("amc,ml->alc", real_two, cos_second, precision=highest) + jnp.einsum(
        "amc,ml->alc", imag_two, sin_second, precision=highest
    )
    imag_out = jnp.einsum("amc,ml->alc", imag_two, cos_second, precision=highest) - jnp.einsum(
        "amc,ml->alc", real_two, sin_second, precision=highest
    )
    return (real_out, imag_out)


def signal(real_in, imag_in):
    first_len, second_len, channels = real_in.shape
    lower_half = first_len // 2
    whole_len = first_len * second_len
    cos_second, sin_second = angle_tables(second_len, second_len, second_len)
    real_one = jnp.einsum("alc,lm->amc", real_in, cos_second, precision=highest) - jnp.einsum(
        "alc,lm->amc", imag_in, sin_second, precision=highest
    )
    imag_one = jnp.einsum("alc,lm->amc", real_in, sin_second, precision=highest) + jnp.einsum(
        "alc,lm->amc", imag_in, cos_second, precision=highest
    )
    twist_cos, twist_sin = angle_tables(first_len, second_len, whole_len)
    twist_cos = twist_cos[:, :, None]
    twist_sin = twist_sin[:, :, None]
    real_two = real_one * twist_cos - imag_one * twist_sin
    imag_two = real_one * twist_sin + imag_one * twist_cos
    cos_first, sin_first = angle_tables(lower_half, first_len, first_len)
    merged = jnp.dot(
        cos_first, real_two.reshape(first_len, second_len * channels), precision=highest
    ) - jnp.dot(sin_first, imag_two.reshape(first_len, second_len * channels), precision=highest)
    return merged.reshape(lower_half * second_len, channels) / whole_len


def complex_product(left_real, left_imag, right_real, right_imag):
    return (
        left_real * right_real - left_imag * right_imag,
        left_real * right_imag + left_imag * right_real,
    )


def conj_product(left_real, left_imag, right_real, right_imag):
    return (
        left_real * right_real + left_imag * right_imag,
        left_imag * right_real - left_real * right_imag,
    )


def times_bf16(left_array, right_array):
    return (left_array.astype(jnp.float32) * right_array.astype(jnp.float32)).astype(jnp.bfloat16)


def body(proj, cotangent, out_weight, short_weight, long_filter):
    tok_rows = proj.shape[0]
    channels = proj.shape[2]
    taps_count = short_weight.shape[0]
    rim_rows = taps_count - 1
    partial_value = lax.dot_general(
        cotangent,
        lax.all_gather(out_weight, "seq", axis=0, tiled=True),
        (((1,), (1,)), ((), ())),
        preferred_element_type=jnp.float32,
    )
    grad_out = lax.psum_scatter(
        partial_value.astype(jnp.bfloat16), "tp", scatter_dimension=1, tiled=True
    )
    lower_rows = shifted(proj[tok_rows - rim_rows :], "seq", 1)
    extended = jnp.concatenate([lower_rows, proj], axis=0)
    primed = short_weight[0] * extended[rim_rows : rim_rows + tok_rows]
    for offset in range(1, taps_count):
        primed = (
            primed
            + short_weight[offset] * extended[rim_rows - offset : rim_rows - offset + tok_rows]
        )
    primed = primed.astype(jnp.bfloat16)
    query_conv = primed[:, 0]
    keys_conv = primed[:, 1]
    value_conv = primed[:, 2]
    gated_input = times_bf16(keys_conv, value_conv)
    filter_cols = lax.all_to_all(
        long_filter.astype(jnp.bfloat16), "seq", split_axis=1, concat_axis=0, tiled=True
    ).astype(long_filter.dtype)
    filter_real, filter_imag = spectrum(filter_cols)
    gated_cols = lax.all_to_all(gated_input, "seq", split_axis=1, concat_axis=0, tiled=True)
    gated_real, gated_imag = spectrum(gated_cols)
    conv_cols = signal(*complex_product(gated_real, gated_imag, filter_real, filter_imag)).astype(
        jnp.bfloat16
    )
    conv_out = lax.all_to_all(conv_cols, "seq", split_axis=0, concat_axis=1, tiled=True)
    grad_query = times_bf16(grad_out, conv_out)
    grad_conv = times_bf16(grad_out, query_conv)
    grad_cols = lax.all_to_all(grad_conv, "seq", split_axis=1, concat_axis=0, tiled=True)
    grad_real, grad_imag = spectrum(grad_cols)
    gated_grad_cols = signal(*conj_product(grad_real, grad_imag, filter_real, filter_imag)).astype(
        jnp.bfloat16
    )
    filter_grad_cols = signal(*conj_product(grad_real, grad_imag, gated_real, gated_imag))
    gated_grad = lax.all_to_all(gated_grad_cols, "seq", split_axis=0, concat_axis=1, tiled=True)
    grad_filter = lax.all_to_all(
        filter_grad_cols.astype(jnp.bfloat16), "seq", split_axis=0, concat_axis=1, tiled=True
    ).astype(filter_grad_cols.dtype)
    grad_keys = times_bf16(gated_grad, value_conv)
    grad_value = times_bf16(gated_grad, keys_conv)
    grad_primed = jnp.stack([grad_query, grad_keys, grad_value], axis=1)
    next_rows = shifted(grad_primed[:rim_rows], "seq", -1)
    trailing = jnp.concatenate([grad_primed, next_rows], axis=0)
    grad_sum = short_weight[0] * trailing[0:tok_rows]
    for offset in range(1, taps_count):
        grad_sum = grad_sum + short_weight[offset] * trailing[offset : offset + tok_rows]
    grad_proj = grad_sum.astype(jnp.bfloat16)
    grad_wide = grad_primed.astype(jnp.float32)
    local_short = jnp.stack(
        [
            jnp.sum(
                grad_wide
                * extended[rim_rows - offset : rim_rows - offset + tok_rows].astype(jnp.float32),
                axis=0,
            )
            for offset in range(taps_count)
        ]
    )
    short_shape = local_short.shape
    grad_short = lax.psum(local_short.reshape(-1, channels), "seq").reshape(short_shape)
    return (grad_proj, grad_short, grad_filter)


def solution(mesh):
    in_specs = (
        P("seq", None, "tp"),
        P("seq", "tp"),
        P("seq", "tp"),
        P(None, None, "tp"),
        P("seq", "tp"),
    )
    out_specs = (P("seq", None, "tp"), P(None, None, "tp"), P("seq", "tp"))
    return jax.shard_map(body, mesh=mesh, in_specs=in_specs, out_specs=out_specs, check_vma=False)
```

profile of v0, /device:TPU:2, one launch (start us, length us, event | category | flops | bytes accessed | tf_op | source)
XLA Modules:
  0.0 583.1 jit_solution(17212374280899392005)
XLA Ops:
  10.5 1.9 copy.45
  12.4 11.3 %all-to-all-start.1 = ((bf16[128,32,32]{0,2,1:T(8,128)(2,1)}), bf16[128,32,32]{0,2,1:T(8,128)(2,1)S(1)}, u32[]{:S(2)}, u32[]{:S(2)}) async-start(bf16[128,32,32]{0,2,1:T(8,128)(2,1)} %bitcast.8), calls=%async_computation.2 | async-start | bytes 524288 | tf_op jit(solution)/shard_map/all_to_all | solution.py:126
  23.9 128.3 %all-gather.2.cloned.1.call-done = bf16[8192,1024]{1,0:T(8,128)(2,1)} async-done(((bf16[256,1024]{1,0:T(8,128)(2,1)}), bf16[8192,1024]{1,0:T(8,128)(2,1)}) %all-gather.2.cloned.1.call-update) | async-done | bytes 16777232 | tf_op jit(solution)/shard_map/all_gather | solution.py:106
  152.2 12.7 %convolution_convert_fusion = bf16[128,8192]{1,0:T(8,128)(2,1)} fusion(bf16[128,1024]{1,0:T(8,128)(2,1)S(1)} %copy-done, bf16[8192,1024]{1,0:T(8,128)(2,1)} %all-gather.2.cloned.1.call-done), kind=kOutput, calls=%fused_computation | convolution fusion | flops 2148532224 | bytes 19136512 | tf_op jit(solution)/shard_map/dot_general | solution.py:104
  168.5 5.8 all-to-all-start
  178.8 2.1 convolution_subtract_fusion.7
  182.1 2.2 convolution_add_fusion.4
  184.3 4.6 all-to-all-done
  193.8 2.2 convolution_subtract_fusion.8
  196.0 22.9 %reduce-scatter.2.cloned.1.call-done = bf16[128,1024]{1,0:T(8,128)(2,1)} async-done(((bf16[128,8192]{1,0:T(8,128)(2,1)}), bf16[128,1024]{1,0:T(8,128)(2,1)}) %reduce-scatter.2.cloned.1.call-update) | async-done | bytes 262160 | tf_op jit(solution)/shard_map/reduce_scatter | solution.py:110
  220.8 9.2 %all-to-all-start.3 = ((bf16[128,32,32]{0,2,1:T(8,128)(2,1)}), bf16[128,32,32]{0,2,1:T(8,128)(2,1)S(1)}, u32[]{:S(2)}, u32[]{:S(2)}) async-start(bf16[128,32,32]{0,2,1:T(8,128)(2,1)} %bitcast.22), calls=%async_computation.4 | async-start | bytes 524288 | tf_op jit(solution)/shard_map/all_to_all | solution.py:138
  231.1 2.1 convolution_add_fusion.5
  233.3 11.4 %all-to-all-done.3 = bf16[128,32,32]{0,2,1:T(8,128)(2,1)S(1)} async-done(((bf16[128,32,32]{0,2,1:T(8,128)(2,1)}), bf16[128,32,32]{0,2,1:T(8,128)(2,1)S(1)}, u32[]{:S(2)}, u32[]{:S(2)}) %all-to-all-start.3) | async-done | bytes 262176 | tf_op jit(solution)/shard_map/all_to_all | solution.py:138
  252.5 2.0 multiply_subtract_fusion.1
  267.6 3.5 multiply_add_fusion
  279.1 4.0 all-to-all-start.2
  290.1 7.6 %all-to-all-done.2 = bf16[32,128,32]{1,2,0:T(8,128)(2,1)S(1)} async-done(((bf16[32,128,32]{1,2,0:T(8,128)(2,1)}), bf16[32,128,32]{1,2,0:T(8,128)(2,1)S(1)}, u32[]{:S(2)}, u32[]{:S(2)}) %all-to-all-start.2) | async-done | bytes 262176 | tf_op jit(solution)/shard_map/all_to_all | solution.py:135
  297.8 4.1 all-to-all-start.4
  301.9 2.6 fusion.168
  307.9 8.4 %all-to-all-done.4 = bf16[32,128,32]{1,2,0:T(8,128)(2,1)S(1)} async-done(((bf16[32,128,32]{1,2,0:T(8,128)(2,1)}), bf16[32,128,32]{1,2,0:T(8,128)(2,1)S(1)}, u32[]{:S(2)}, u32[]{:S(2)}) %all-to-all-start.4) | async-done | bytes 262176 | tf_op jit(solution)/shard_map/all_to_all | solution.py:144
  316.3 3.9 all-to-all-start.5
  325.4 9.4 %all-to-all-done.5 = bf16[32,128,32]{1,2,0:T(8,128)(2,1)S(1)} async-done(((bf16[32,128,32]{1,2,0:T(8,128)(2,1)}), bf16[32,128,32]{1,2,0:T(8,128)(2,1)S(1)}, u32[]{:S(2)}, u32[]{:S(2)}) %all-to-all-start.5) | async-done | bytes 262176 | tf_op jit(solution)/shard_map/all_to_all | solution.py:145
  336.1 2.3 fusion.19
  338.4 236.1 %all-reduce.2.cloned.1.call-done = f32[7,3,1024]{2,1,0:T(4,128)} async-done(((f32[7,3,1024]{2,1,0:T(4,128)}), f32[7,3,1024]{2,1,0:T(4,128)}) %all-reduce.2.cloned.1.call-update) | async-done | bytes 86032 | tf_op jit(solution)/shard_map/psum | solution.py:169
  (137 shorter events, 67.6 us)
Async XLA Ops:
  7.2 145.0 %copy-start = (bf16[128,1024]{1,0:T(8,128)(2,1)S(1)}, bf16[128,1024]{1,0:T(8,128)(2,1)}, u32[]{:S(2)}) copy-start(bf16[128,1024]{1,0:T(8,128)(2,1)} %param.6) | copy-start | bytes 786436
  7.2 16.6 %copy-start.21 = (f32[7,3,1024]{2,0,1:T(8,128)S(1)}, f32[7,3,1024]{2,0,1:T(8,128)}, u32[]{:S(2)}) copy-start(f32[7,3,1024]{2,0,1:T(8,128)} %param.8) | copy-start | bytes 258052
  7.2 145.0 %all-gather.2.cloned.1.call-start = ((), (), s32[]{:S(2)}) async-start(), calls=%async_computation.7 | async-start | bytes 17301504 | tf_op jit(solution)/shard_map/all_gather | solution.py:106
  8.7 156.4 %collective-permute-start = (bf16[6,3,1024]{2,0,1:T(8,128)(2,1)S(1)}, bf16[6,3,1024]{2,0,1:T(8,128)(2,1)S(1)}, u32[]{:S(2)}, u32[]{:S(2)}) collective-permute-start(bf16[6,3,1024]{2,0,1:T(8,128)(2,1)S(1)} %slice.87), channel_id=1, source_target_pairs={{0,8},{8,16},{16,24},{24,32},{32,40},{40,48},{48,56},{56,64},{64,7... | collective-permute-start | bytes 110600 | tf_op jit(solution)/shard_map/ppermute | solution.py:13
  12.4 156.1 %all-to-all-start.1 = ((bf16[128,32,32]{0,2,1:T(8,128)(2,1)}), bf16[128,32,32]{0,2,1:T(8,128)(2,1)S(1)}, u32[]{:S(2)}, u32[]{:S(2)}) async-start(bf16[128,32,32]{0,2,1:T(8,128)(2,1)} %bitcast.8), calls=%async_computation.2 | async-start | bytes 524288 | tf_op jit(solution)/shard_map/all_to_all | solution.py:126
  23.7 195.2 %reduce-scatter.2.cloned.1.call-start = ((), (), s32[]{:S(2)}) async-start(), calls=%async_computation.8 | async-start | bytes 2359296 | tf_op jit(solution)/shard_map/reduce_scatter | solution.py:110
  165.0 3.5 copy-start.11
  165.0 3.5 copy-start.13
  165.0 3.5 copy-start.15
  165.0 3.5 copy-start.17
  165.2 3.3 copy-start.19
  168.5 20.3 %all-to-all-start = ((bf16[128,32,32]{0,2,1:T(8,128)(2,1)}), bf16[128,32,32]{0,2,1:T(8,128)(2,1)S(1)}, u32[]{:S(2)}, u32[]{:S(2)}) async-start(bf16[128,32,32]{0,2,1:T(8,128)(2,1)} %bitcast.2), calls=%async_computation.1 | async-start | bytes 524288 | tf_op jit(solution)/shard_map/all_to_all | solution.py:130
  220.8 23.9 %all-to-all-start.3 = ((bf16[128,32,32]{0,2,1:T(8,128)(2,1)}), bf16[128,32,32]{0,2,1:T(8,128)(2,1)S(1)}, u32[]{:S(2)}, u32[]{:S(2)}) async-start(bf16[128,32,32]{0,2,1:T(8,128)(2,1)} %bitcast.22), calls=%async_computation.4 | async-start | bytes 524288 | tf_op jit(solution)/shard_map/all_to_all | solution.py:138
  250.4 1.5 copy-start.3
  250.4 1.8 copy-start.4
  250.4 2.1 copy-start.5
  279.1 5.9 %copy-start.6 = (f32[128,64,32]{0,1,2:T(8,128)S(1)}, f32[128,64,32]{0,1,2:T(8,128)}, u32[]{:S(2)}) copy-start(f32[128,64,32]{0,1,2:T(8,128)} %get-tuple-element.48) | copy-start | bytes 3145732
  279.1 18.7 %all-to-all-start.2 = ((bf16[32,128,32]{1,2,0:T(8,128)(2,1)}), bf16[32,128,32]{1,2,0:T(8,128)(2,1)S(1)}, u32[]{:S(2)}, u32[]{:S(2)}) async-start(bf16[32,128,32]{1,2,0:T(8,128)(2,1)} %copy.52), calls=%async_computation.3 | async-start | bytes 524288 | tf_op jit(solution)/shard_map/all_to_all | solution.py:135
  297.8 18.5 %all-to-all-start.4 = ((bf16[32,128,32]{1,2,0:T(8,128)(2,1)}), bf16[32,128,32]{1,2,0:T(8,128)(2,1)S(1)}, u32[]{:S(2)}, u32[]{:S(2)}) async-start(bf16[32,128,32]{1,2,0:T(8,128)(2,1)} %copy.61), calls=%async_computation.5 | async-start | bytes 524288 | tf_op jit(solution)/shard_map/all_to_all | solution.py:144
  316.3 18.5 %all-to-all-start.5 = ((bf16[32,128,32]{1,2,0:T(8,128)(2,1)}), bf16[32,128,32]{1,2,0:T(8,128)(2,1)S(1)}, u32[]{:S(2)}, u32[]{:S(2)}) async-start(bf16[32,128,32]{1,2,0:T(8,128)(2,1)} %copy.66), calls=%async_computation.6 | async-start | bytes 524288 | tf_op jit(solution)/shard_map/all_to_all | solution.py:145
  320.2 254.4 %all-reduce.2.cloned.1.call-start = ((), (), s32[]{:S(2)}) async-start(), calls=%async_computation.9 | async-start | bytes 229376 | tf_op jit(solution)/shard_map/psum | solution.py:169
  324.0 11.9 %collective-permute-start.1 = (bf16[6,3,1024]{2,0,1:T(8,128)(2,1)S(1)}, bf16[6,3,1024]{2,0,1:T(8,128)(2,1)S(1)}, u32[]{:S(2)}, u32[]{:S(2)}) collective-permute-start(bf16[6,3,1024]{2,0,1:T(8,128)(2,1)S(1)} %slice.122), channel_id=1, source_target_pairs={{8,0},{16,8},{24,16},{32,24},{40,32},{48,40},{56,48},{64,56},{72,6... | collective-permute-start | bytes 110600 | tf_op jit(solution)/shard_map/ppermute | solution.py:13
  325.4 10.5 %copy-start.10 = (f32[7,3,1024]{2,1,0:T(4,128)}, f32[7,3,1024]{2,1,0:T(4,128)S(1)}, u32[]{:S(2)}) copy-start(f32[7,3,1024]{2,1,0:T(4,128)S(1)} %constant_dynamic-update-slice_fusion) | copy-start | bytes 258052
  336.1 240.0 %copy-start.1 = (bf16[128,1024]{1,0:T(8,128)(2,1)S(1)}, bf16[128,1024]{1,0:T(8,128)(2,1)}, u32[]{:S(2)}) copy-start(bf16[128,1024]{1,0:T(8,128)(2,1)} %param.6) | copy-start | bytes 786436
  (9 other events, 10.3 us)
Sparse Core Ops, SparseCore 0:
  10.8 141.3 all-gather.1
  165.1 53.7 reduce-scatter.1
  336.1 238.4 all-reduce.1
where the time goes:
time: 589 us; the launch traced here: 583 us
  waiting for transfers between devices  429 us (73%)
  matrix products  62.1 us (11%)
  starting transfers between devices  41.5 us (7%)
  local copies, waits for them, and re-layouts  27.9 us (5%)
  between operations  15 us (3%)
  other arithmetic  7.24 us (1%)
    psum x1, waiting for transfers between devices, body(): lax.psum(local_short.reshape(-1, channels), 'seq').reshape(short_shape)  236 us
    all_gather x1, waiting for transfers between devices, body(): lax.all_gather(out_weight, 'seq', axis=0, tiled=True)  128 us
    reduce_scatter x1, waiting for transfers between devices, body(): lax.psum_scatter(partial_value.astype(jnp.bfloat16), 'tp', scatter_dimens...  22.9 us
    dot_general x1, matrix products, body(): lax.dot_general(cotangent, lax.all_gather(out_weight, 'seq', axis=0, tile...  12.7 us
  transfers between devices with their start and end apart: 11, of which 8 were waited for; matrix products, arithmetic and copies ran while one was open for 10% of the time, Pallas kernels for 0%

commit v1 on v0

--- a/solution.py
+++ b/solution.py
@@ -103,7 +103,9 @@
     rim_rows = taps_count - 1
     partial_value = lax.dot_general(
         cotangent,
-        lax.all_gather(out_weight, "seq", axis=0, tiled=True),
+        jnp.concatenate(
+            lax.all_to_all(jnp.stack([out_weight] * lax.axis_size("seq")), "seq", 0, 0), axis=0
+        ),
         (((1,), (1,)), ((), ())),
         preferred_element_type=jnp.float32,
     )

time: 589 us -> 847 us (1.44)
  waiting for transfers between devices: 429 us -> 669 us
  starting transfers between devices: 41.5 us -> 54.5 us
    all_to_all x0 -> x1, waiting for transfers between devices: none -> 368 us  [body(): lax.all_to_all(jnp.stack([out_weight] * lax.axis_size('seq')), 'seq', 0, 0)]
    all_gather x1 -> x0, waiting for transfers between devices: 128 us -> none  [body(): lax.all_gather(out_weight, 'seq', axis=0, tiled=True)]
    all_to_all x0 -> x1, starting transfers between devices: none -> 10.7 us  [body(): lax.all_to_all(jnp.stack([out_weight] * lax.axis_size('seq')), 'seq', 0, 0)]
  transfers between devices with their start and end apart: 11 -> 11, of which waited for: 8 -> 8; matrix products, arithmetic and copies ran while one was open for 10% -> 7% of each run, Pallas kernels for 0% -> 0%
where the time goes in v1:
time: 847 us; the launch traced here: 840 us
  waiting for transfers between devices  669 us (79%)
  matrix products  62.1 us (7%)
  starting transfers between devices  54.5 us (6%)
  local copies, waits for them, and re-layouts  32 us (4%)
  between operations  15.3 us (2%)
    all_to_all x1, waiting for transfers between devices, body(): lax.all_to_all(jnp.stack([out_weight] * lax.axis_size('seq')), 'seq', 0, 0)  368 us
    psum x1, waiting for transfers between devices, body(): lax.psum(local_short.reshape(-1, channels), 'seq').reshape(short_shape)  236 us
    reduce_scatter x1, waiting for transfers between devices, body(): lax.psum_scatter(partial_value.astype(jnp.bfloat16), 'tp', scatter_dimens...  24.2 us
  transfers between devices with their start and end apart: 11, of which 8 were waited for; matrix products, arithmetic and copies ran while one was open for 7% of the time, Pallas kernels for 0%

profile of v1, /device:TPU:2, one launch (start us, length us, event | category | flops | bytes accessed | tf_op | source)
XLA Modules:
  0.0 840.5 jit_solution(10240156548089646198)
XLA Ops:
  7.2 6.8 stack.22
  14.0 10.7 %all-to-all-start = ((bf16[32,256,1024]{2,1,0:T(8,128)(2,1)}), bf16[32,256,1024]{2,1,0:T(8,128)(2,1)}, u32[]{:S(2)}, u32[]{:S(2)}) async-start(bf16[32,256,1024]{2,1,0:T(8,128)(2,1)} %stack.22), calls=%async_computation | async-start | bytes 33554432 | tf_op jit(solution)/shard_map/all_to_all | solution.py:107
  27.8 367.6 %all-to-all-done = bf16[32,256,1024]{2,1,0:T(8,128)(2,1)} async-done(((bf16[32,256,1024]{2,1,0:T(8,128)(2,1)}), bf16[32,256,1024]{2,1,0:T(8,128)(2,1)}, u32[]{:S(2)}, u32[]{:S(2)}) %all-to-all-start) | async-done | bytes 16777248 | tf_op jit(solution)/shard_map/all_to_all | solution.py:107
  395.4 9.1 %all-to-all-start.2 = ((bf16[128,32,32]{0,2,1:T(8,128)(2,1)}), bf16[128,32,32]{0,2,1:T(8,128)(2,1)S(1)}, u32[]{:S(2)}, u32[]{:S(2)}) async-start(bf16[128,32,32]{0,2,1:T(8,128)(2,1)} %bitcast.9), calls=%async_computation.3 | async-start | bytes 524288 | tf_op jit(solution)/shard_map/all_to_all | solution.py:128
  404.5 12.7 %convolution_convert_fusion = bf16[128,8192]{1,0:T(8,128)(2,1)} fusion(bf16[128,1024]{1,0:T(8,128)(2,1)S(1)} %copy-done, bf16[8192,1024]{1,0:T(8,128)(2,1)} %bitcast), kind=kOutput, calls=%fused_computation | convolution fusion | flops 2148532224 | bytes 19136512 | tf_op jit(solution)/shard_map/dot_general | solution.py:104
  420.0 10.0 %all-to-all-start.1 = ((bf16[128,32,32]{0,2,1:T(8,128)(2,1)}), bf16[128,32,32]{0,2,1:T(8,128)(2,1)S(1)}, u32[]{:S(2)}, u32[]{:S(2)}) async-start(bf16[128,32,32]{0,2,1:T(8,128)(2,1)} %bitcast.3), calls=%async_computation.2 | async-start | bytes 524288 | tf_op jit(solution)/shard_map/all_to_all | solution.py:132
  434.6 2.2 convolution_add_fusion.4
  437.9 2.1 convolution_subtract_fusion.7
  440.0 4.6 all-to-all-done.1
  449.6 2.2 convolution_add_fusion.5
  451.8 24.2 %reduce-scatter.2.cloned.1.call-done = bf16[128,1024]{1,0:T(8,128)(2,1)} async-done(((bf16[128,8192]{1,0:T(8,128)(2,1)}), bf16[128,1024]{1,0:T(8,128)(2,1)}) %reduce-scatter.2.cloned.1.call-update) | async-done | bytes 262160 | tf_op jit(solution)/shard_map/reduce_scatter | solution.py:112
  477.8 9.2 %all-to-all-start.4 = ((bf16[128,32,32]{0,2,1:T(8,128)(2,1)}), bf16[128,32,32]{0,2,1:T(8,128)(2,1)S(1)}, u32[]{:S(2)}, u32[]{:S(2)}) async-start(bf16[128,32,32]{0,2,1:T(8,128)(2,1)} %bitcast.23), calls=%async_computation.5 | async-start | bytes 524288 | tf_op jit(solution)/shard_map/all_to_all | solution.py:140
  488.2 2.1 convolution_subtract_fusion.8
  490.3 11.3 %all-to-all-done.4 = bf16[128,32,32]{0,2,1:T(8,128)(2,1)S(1)} async-done(((bf16[128,32,32]{0,2,1:T(8,128)(2,1)}), bf16[128,32,32]{0,2,1:T(8,128)(2,1)S(1)}, u32[]{:S(2)}, u32[]{:S(2)}) %all-to-all-start.4) | async-done | bytes 262176 | tf_op jit(solution)/shard_map/all_to_all | solution.py:140
  524.6 3.5 multiply_add_fusion
  536.1 4.0 all-to-all-start.3
  547.2 7.6 all-to-all-done.3
  554.8 4.1 all-to-all-start.5
  558.9 2.6 fusion.168
  565.0 8.4 all-to-all-done.5
  573.3 3.9 all-to-all-start.6
  582.5 9.4 %all-to-all-done.6 = bf16[32,128,32]{1,2,0:T(8,128)(2,1)S(1)} async-done(((bf16[32,128,32]{1,2,0:T(8,128)(2,1)}), bf16[32,128,32]{1,2,0:T(8,128)(2,1)S(1)}, u32[]{:S(2)}, u32[]{:S(2)}) %all-to-all-start.6) | async-done | bytes 262176 | tf_op jit(solution)/shard_map/all_to_all | solution.py:147
  593.1 2.3 fusion.19
  595.4 236.2 %all-reduce.2.cloned.1.call-done = f32[7,3,1024]{2,1,0:T(4,128)} async-done(((f32[7,3,1024]{2,1,0:T(4,128)}), f32[7,3,1024]{2,1,0:T(4,128)}) %all-reduce.2.cloned.1.call-update) | async-done | bytes 86032 | tf_op jit(solution)/shard_map/psum | solution.py:171
  (139 shorter events, 68.5 us)
Async XLA Ops:
  7.2 397.3 %copy-start = (bf16[128,1024]{1,0:T(8,128)(2,1)S(1)}, bf16[128,1024]{1,0:T(8,128)(2,1)}, u32[]{:S(2)}) copy-start(bf16[128,1024]{1,0:T(8,128)(2,1)} %param.6) | copy-start | bytes 786436
  14.0 10.7 %copy-start.7 = (bf16[128,3,1024]{2,0,1:T(8,128)(2,1)S(1)}, bf16[128,3,1024]{2,0,1:T(8,128)(2,1)}, u32[]{:S(2)}) copy-start(bf16[128,3,1024]{2,0,1:T(8,128)(2,1)} %param.5) | copy-start | bytes 2359300
  14.0 12.9 %copy-start.10 = (f32[128,1024]{1,0:T(8,128)S(1)}, f32[128,1024]{1,0:T(8,128)}, u32[]{:S(2)}) copy-start(f32[128,1024]{1,0:T(8,128)} %param.9) | copy-start | bytes 1572868
  14.0 13.7 %copy-start.22 = (f32[7,3,1024]{2,0,1:T(8,128)S(1)}, f32[7,3,1024]{2,0,1:T(8,128)}, u32[]{:S(2)}) copy-start(f32[7,3,1024]{2,0,1:T(8,128)} %param.8) | copy-start | bytes 258052
  14.0 381.3 %all-to-all-start = ((bf16[32,256,1024]{2,1,0:T(8,128)(2,1)}), bf16[32,256,1024]{2,1,0:T(8,128)(2,1)}, u32[]{:S(2)}, u32[]{:S(2)}) async-start(bf16[32,256,1024]{2,1,0:T(8,128)(2,1)} %stack.22), calls=%async_computation | async-start | bytes 33554432 | tf_op jit(solution)/shard_map/all_to_all | solution.py:107
  24.7 392.8 %collective-permute-start = (bf16[6,3,1024]{2,0,1:T(8,128)(2,1)S(1)}, bf16[6,3,1024]{2,0,1:T(8,128)(2,1)S(1)}, u32[]{:S(2)}, u32[]{:S(2)}) collective-permute-start(bf16[6,3,1024]{2,0,1:T(8,128)(2,1)S(1)} %slice.87), channel_id=1, source_target_pairs={{0,8},{8,16},{16,24},{24,32},{32,40},{40,48},{48,56},{56,64},{64,7... | collective-permute-start | bytes 110600 | tf_op jit(solution)/shard_map/ppermute | solution.py:13
  395.4 24.6 %all-to-all-start.2 = ((bf16[128,32,32]{0,2,1:T(8,128)(2,1)}), bf16[128,32,32]{0,2,1:T(8,128)(2,1)S(1)}, u32[]{:S(2)}, u32[]{:S(2)}) async-start(bf16[128,32,32]{0,2,1:T(8,128)(2,1)} %bitcast.9), calls=%async_computation.3 | async-start | bytes 524288 | tf_op jit(solution)/shard_map/all_to_all | solution.py:128
  404.5 71.5 %reduce-scatter.2.cloned.1.call-start = ((), (), s32[]{:S(2)}) async-start(), calls=%async_computation.8 | async-start | bytes 2359296 | tf_op jit(solution)/shard_map/reduce_scatter | solution.py:112
  417.3 2.7 copy-start.12
  417.3 2.7 copy-start.14
  417.3 2.7 copy-start.16
  417.3 2.6 copy-start.18
  417.5 2.5 copy-start.20
  420.0 24.6 %all-to-all-start.1 = ((bf16[128,32,32]{0,2,1:T(8,128)(2,1)}), bf16[128,32,32]{0,2,1:T(8,128)(2,1)S(1)}, u32[]{:S(2)}, u32[]{:S(2)}) async-start(bf16[128,32,32]{0,2,1:T(8,128)(2,1)} %bitcast.3), calls=%async_computation.2 | async-start | bytes 524288 | tf_op jit(solution)/shard_map/all_to_all | solution.py:132
  477.8 23.9 %all-to-all-start.4 = ((bf16[128,32,32]{0,2,1:T(8,128)(2,1)}), bf16[128,32,32]{0,2,1:T(8,128)(2,1)S(1)}, u32[]{:S(2)}, u32[]{:S(2)}) async-start(bf16[128,32,32]{0,2,1:T(8,128)(2,1)} %bitcast.23), calls=%async_computation.5 | async-start | bytes 524288 | tf_op jit(solution)/shard_map/all_to_all | solution.py:140
  507.4 2.1 copy-start.5
  536.1 5.9 copy-start.6
  536.1 18.7 %all-to-all-start.3 = ((bf16[32,128,32]{1,2,0:T(8,128)(2,1)}), bf16[32,128,32]{1,2,0:T(8,128)(2,1)S(1)}, u32[]{:S(2)}, u32[]{:S(2)}) async-start(bf16[32,128,32]{1,2,0:T(8,128)(2,1)} %copy.52), calls=%async_computation.4 | async-start | bytes 524288 | tf_op jit(solution)/shard_map/all_to_all | solution.py:137
  554.8 18.5 %all-to-all-start.5 = ((bf16[32,128,32]{1,2,0:T(8,128)(2,1)}), bf16[32,128,32]{1,2,0:T(8,128)(2,1)S(1)}, u32[]{:S(2)}, u32[]{:S(2)}) async-start(bf16[32,128,32]{1,2,0:T(8,128)(2,1)} %copy.61), calls=%async_computation.6 | async-start | bytes 524288 | tf_op jit(solution)/shard_map/all_to_all | solution.py:146
  573.3 18.5 %all-to-all-start.6 = ((bf16[32,128,32]{1,2,0:T(8,128)(2,1)}), bf16[32,128,32]{1,2,0:T(8,128)(2,1)S(1)}, u32[]{:S(2)}, u32[]{:S(2)}) async-start(bf16[32,128,32]{1,2,0:T(8,128)(2,1)} %copy.66), calls=%async_computation.7 | async-start | bytes 524288 | tf_op jit(solution)/shard_map/all_to_all | solution.py:147
  577.2 254.4 %all-reduce.2.cloned.1.call-start = ((), (), s32[]{:S(2)}) async-start(), calls=%async_computation.9 | async-start | bytes 229376 | tf_op jit(solution)/shard_map/psum | solution.py:171
  581.0 11.9 %collective-permute-start.1 = (bf16[6,3,1024]{2,0,1:T(8,128)(2,1)S(1)}, bf16[6,3,1024]{2,0,1:T(8,128)(2,1)S(1)}, u32[]{:S(2)}, u32[]{:S(2)}) collective-permute-start(bf16[6,3,1024]{2,0,1:T(8,128)(2,1)S(1)} %slice.122), channel_id=1, source_target_pairs={{8,0},{16,8},{24,16},{32,24},{40,32},{48,40},{56,48},{64,56},{72,6... | collective-permute-start | bytes 110600 | tf_op jit(solution)/shard_map/ppermute | solution.py:13
  582.4 10.5 %copy-start.11 = (f32[7,3,1024]{2,1,0:T(4,128)}, f32[7,3,1024]{2,1,0:T(4,128)S(1)}, u32[]{:S(2)}) copy-start(f32[7,3,1024]{2,1,0:T(4,128)S(1)} %constant_dynamic-update-slice_fusion) | copy-start | bytes 258052
  593.1 240.1 %copy-start.1 = (bf16[128,1024]{1,0:T(8,128)(2,1)S(1)}, bf16[128,1024]{1,0:T(8,128)(2,1)}, u32[]{:S(2)}) copy-start(bf16[128,1024]{1,0:T(8,128)(2,1)} %param.6) | copy-start | bytes 786436
  (10 other events, 12.5 us)
Sparse Core Ops, SparseCore 0:
  417.4 58.5 reduce-scatter.1
  593.1 238.4 all-reduce.1
